TPU v7x, 512 devices: a whole 4x4x16 slice. The times are simulated.
512 devices in a mesh: req: 128 (over z, x, core), tp: 4 (over y).
Axes of the slice: x: 4, y: 4, z: 16, core: 2. Of those that a mesh axis runs over, the one named last changes fastest.
Arguments:
- queries: bfloat16 [16384, 3584], P('req', 'tp'), may hold values from -13 to 13
- tree_kv: bfloat16 [16384, 4, 256], P('req', 'tp'), may hold values from -5 to 5
- page_pool: bfloat16 [1536, 4, 128, 256], P('req', 'tp'), may hold values from -5 to 5
- page_table: int32 [256, 8], P('req'), may hold values from 0 to 11, as said below
- cache_len: int32 [256], P('req'), may hold values from 1 to 1024
- parents: int32 [256, 64], P('req'), may hold values from -1 to 62, as said below
- accepted: int32 [256], P('req'), may hold values from 0 to 63
- o_weight: bfloat16 [3584, 1792], P('tp'), may hold values from -0.5 to 0.5
Outputs:
- projected: bfloat16 [16384, 1792], P(('req', 'tp'))
- kept_rows: bfloat16 [16384, 4, 256], P('req', 'tp')
Inputs may be any that keep to these rules, and one draw needn't show every extreme that they name: Logical page k of request r is in slot page_table[r, k] of its own device's pool for k < 2, among that pool's first 4 slots, and for k >= 2 in that slot of the next req device's pool (the first device after the last), among its last 8 slots; distinct pages are in distinct slots; entries at k >= ceil(cache_len[r] / 128) are 0. parents[r, 0] = -1 and 0 <= parents[r, j] < j for j >= 1.
All inputs are finite; a program needn't handle non-finite values.
Results may differ from a plain program's by a relative error of at most 0.007.
Values may be sent and summed in bfloat16 or wider, within the bound.
No kernel may reach another device: no remote copies, remote signals or barrier semaphores. Data moves between devices by JAX's collectives and lax.ppermute only.
A program may use at most 64 MiB of HBM per device.

v0:
```python
import math
import jax
import jax.numpy as jnp
from jax import lax
from jax.sharding import PartitionSpec as P

HEAD_SIZE = 128
LOCAL = 2
very_negative = -1e30


def from_behind(block, axis, distance):
    devices = range(lax.axis_size(axis))
    route = [((i - distance) % len(devices), i) for i in devices]
    return lax.ppermute(block, axis, route)


def ancestors(parent_row):
    tree_len = parent_row.shape[0]
    node_ids = jnp.arange(tree_len, dtype=jnp.int32)
    parent_links = (parent_row[:, None] == node_ids[None, :]).astype(jnp.float32)
    reachable = jnp.eye(tree_len, dtype=jnp.float32) + parent_links
    for squaring in range((tree_len - 1).bit_length()):
        reachable = jnp.minimum(jnp.dot(reachable, reachable, precision=lax.Precision.HIGHEST), 1.0)
    return reachable


def block_stats(query_rows, block_keys, block_values, visible):
    scores = jnp.einsum(
        "tgd,nd->tgn", query_rows, block_keys, preferred_element_type=jnp.float32
    ) * (1.0 / math.sqrt(query_rows.shape[-1]))
    scores = jnp.where(visible, scores, very_negative)
    maxima = jnp.max(scores, axis=-1)
    weights = jnp.where(visible, jnp.exp(scores - maxima[..., None]), 0.0).astype(jnp.bfloat16)
    totals = jnp.sum(weights.astype(jnp.float32), axis=-1)
    accums = jnp.einsum("tgn,nd->tgd", weights, block_values, preferred_element_type=jnp.float32)
    return (maxima, totals, accums)


def combine(first_state, second_state):
    joined_max = jnp.maximum(first_state[0], second_state[0])
    first_factor = jnp.exp(first_state[0] - joined_max)
    second_factor = jnp.exp(second_state[0] - joined_max)
    totals = first_factor * first_state[1] + second_factor * second_state[1]
    accums = first_factor[..., None] * first_state[2] + second_factor[..., None] * second_state[2]
    return (joined_max, totals, accums)


def pages_partial(query_rows, pages, visible):
    head_dim = query_rows.shape[-1]
    scores = jnp.einsum(
        "tgd,knd->tgkn", query_rows, pages[..., :head_dim], preferred_element_type=jnp.float32
    ) * (1.0 / math.sqrt(head_dim))
    mask = visible[None, None, :, :]
    scores = jnp.where(mask, scores, very_negative)
    maxima = jnp.max(scores, axis=-1)
    weights = jnp.where(mask, jnp.exp(scores - maxima[..., None]), 0.0).astype(jnp.bfloat16)
    totals = jnp.sum(weights.astype(jnp.float32), axis=-1)
    accums = jnp.einsum(
        "tgkn,knd->tgkd", weights, pages[..., head_dim:], preferred_element_type=jnp.float32
    )
    overall = jnp.max(maxima, axis=-1)
    factors = jnp.exp(maxima - overall[..., None])
    total = jnp.sum(factors * totals, axis=-1)
    accum = jnp.sum(factors[..., None] * accums, axis=2)
    return (overall, total, accum)


def sweep_all(query_rows, pool_slots, tables, lengths, first_page):
    page_len = pool_slots.shape[1]
    page_count = tables.shape[1]
    offsets = jnp.arange(page_len, dtype=jnp.int32)
    page_numbers = first_page + jnp.arange(page_count, dtype=jnp.int32)
    positions = page_numbers[:, None] * page_len + offsets[None, :]

    def one_request(request_data):
        request_query, table_row, length = request_data
        pages = jnp.take(pool_slots, table_row, axis=0)
        visible = positions < length
        return pages_partial(request_query, pages, visible)

    return lax.map(one_request, (query_rows, tables, lengths))


def shards(queries, tree_kv, page_pool, page_table, cache_len, parents, accepted, o_weight):
    requests = page_table.shape[0]
    tree_len = parents.shape[1]
    group_size = queries.shape[1] // HEAD_SIZE
    query_rows = queries.reshape(requests, tree_len, group_size, HEAD_SIZE)
    tree_rows = tree_kv[:, 0, :].reshape(requests, tree_len, 2 * HEAD_SIZE)
    pool_slots = page_pool[:, 0]
    reachable = jax.vmap(ancestors)(parents)
    page_meta = jnp.concatenate([page_table, cache_len[:, None]], axis=1)
    moved_queries, moved_meta = from_behind((queries, page_meta), "req", 1)
    moved_rows = moved_queries.reshape(requests, tree_len, group_size, HEAD_SIZE)
    partial_value = sweep_all(
        moved_rows, pool_slots, moved_meta[:, LOCAL:-1], moved_meta[:, -1], LOCAL
    )
    returned = from_behind((partial_value[2], partial_value[0], partial_value[1]), "req", -1)
    local_state = sweep_all(query_rows, pool_slots, page_table[:, :LOCAL], cache_len, 0)
    page_state = combine(local_state, (returned[1], returned[2], returned[0]))
    tree_visible = (reachable > 0.5)[:, :, None, :]
    tree_state = jax.vmap(block_stats)(
        query_rows, tree_rows[:, :, :HEAD_SIZE], tree_rows[:, :, HEAD_SIZE:], tree_visible
    )
    merged = combine(page_state, tree_state)
    attention = (
        (merged[2] / merged[1][..., None])
        .astype(jnp.bfloat16)
        .reshape(requests * tree_len, group_size * HEAD_SIZE)
    )
    rows_out = attention.shape[0] // lax.axis_size("tp")
    whole_sum = lax.psum(jnp.dot(attention, o_weight, preferred_element_type=jnp.float32), "tp")
    summed = lax.dynamic_slice_in_dim(whole_sum, lax.axis_index("tp") * rows_out, rows_out, 0)
    projected = summed.astype(jnp.bfloat16)
    node_ids = jnp.arange(tree_len, dtype=jnp.int32)
    leaf_onehot = (accepted[:, None] == node_ids[None, :]).astype(jnp.float32)
    kept_mask = jnp.einsum("rm,rmn->rn", leaf_onehot, reachable, precision=lax.Precision.HIGHEST)
    depths = jnp.sum(reachable, axis=2) - 1.0
    slot_ids = jnp.arange(tree_len, dtype=jnp.float32)
    selector = (
        kept_mask[:, None, :] * (depths[:, None, :] == slot_ids[None, :, None]).astype(jnp.float32)
    ).astype(jnp.bfloat16)
    kept = jnp.einsum(
        "rsm,rmc->rsc", selector, tree_rows, preferred_element_type=jnp.float32
    ).astype(jnp.bfloat16)
    return (projected, kept.reshape(requests * tree_len, 1, 2 * HEAD_SIZE))


def solution(mesh):
    in_specs = (
        P("req", "tp"),
        P("req", "tp", None),
        P("req", "tp", None, None),
        P("req", None),
        P("req"),
        P("req", None),
        P("req"),
        P("tp", None),
    )
    out_specs = (P(("req", "tp"), None), P("req", "tp", None))
    return jax.shard_map(shards, mesh=mesh, in_specs=in_specs, out_specs=out_specs, check_vma=False)
```

profile of v0, /device:TPU:8, one launch (start us, length us, event | category | flops | bytes accessed | tf_op | source)
XLA Modules:
  0.0 122.9 jit_solution(13484984771491410831)
XLA Ops:
  1.5 1.4 %pad_add_fusion = s32[2,9]{1,0:T(2,128)} fusion(s32[2,1]{1,0:T(2,128)S(1)} %copy.48, s32[2,8]{1,0:T(2,128)} %param.15), kind=kLoop, calls=%fused_computation.98 | loop fusion | flops 18 | bytes 144 | tf_op jit(solution)/shard_map/concatenate | solution.py:93
  2.9 1.9 %collective-permute-start = (s32[2,9]{1,0:T(2,128)}, s32[2,9]{1,0:T(2,128)}, u32[]{:S(2)}, u32[]{:S(2)}) collective-permute-start(s32[2,9]{1,0:T(2,128)} %pad_add_fusion), channel_id=1, source_target_pairs={{508,0},{0,4},{4,8},{8,12},{12,16},{16,20},{20,24},{24,28},{28,32}... | collective-permute-start | bytes 224 | tf_op jit(solution)/shard_map/ppermute | solution.py:15
  4.8 3.5 %collective-permute-start.1 = (bf16[128,896]{1,0:T(8,128)(2,1)}, bf16[128,896]{1,0:T(8,128)(2,1)}, u32[]{:S(2)}, u32[]{:S(2)}) collective-permute-start(bf16[128,896]{1,0:T(8,128)(2,1)} %param.12), channel_id=1, source_target_pairs={{508,0},{0,4},{4,8},{8,12},{12,16},{16,20},{20,24},{24,28},{28,32}... | collective-permute-start | bytes 688136 | tf_op jit(solution)/shard_map/ppermute | solution.py:15
  15.6 1.4 %fusion.35 = f32[2,1,64]{2,1,0:T(1,128)} fusion(f32[2,64,64]{2,1,0:T(8,128)S(1)} %get-tuple-element.262, pred[2,64,1]{1,0,2:T(4,128)(4,1)} %compare_bitcast_fusion), kind=kOutput, calls=%fused_computation.95 | convolution fusion | flops 98304 | bytes 33408 | tf_op jit(solution)/shard_map/rm,rmn->rn/dot_general | solution.py:118
  18.5 17.2 %while.30 = (s32[]{:T(128)}, f32[2,64,7]{1,2,0:T(8,128)S(1)}, f32[2,64,7]{1,2,0:T(8,128)S(1)}, f32[2,64,7,128]{3,1,2,0:T(8,128)}, s32[2]{0:T(128)}, /*index=5*/b...) while((s32[]{:T(128)}, f32[2,64,7]{1,2,0:T(8,128)S(1)}, ...), condition=%wide.region_6.7_spmd.clone, body=%wide.region_0.6_spmd.clone.sunk | while | flops 59991572 | bytes 6568445 | solution.py:82
  22.5 1.7 %gather_fusion = bf16[2,128,256]{2,1,0:T(8,128)(2,1)S(1)} fusion(bf16[12,128,256]{2,1,0:T(8,128)(2,1)} %get-tuple-element.468, s32[1024]{0:T(1024)S(1)} %pad_clamp_fusion.4), kind=kCustom, calls=%fused_computation.clone.clone.1 | custom fusion | bytes 262152 | tf_op jit(solution)/shard_map/while/body/eval_jaxpr/jit(_take)/gather | solution.py:78
  24.3 1.4 %fusion.68 = (f32[64,7,2]{0,2,1:T(2,128)S(1)}, f32[64,7]{0,1:T(8,128)S(1)}, f32[64,7,2,128]{3,0,2,1:T(8,128)S(1)}) fusion(bf16[2,128,256]{2,1,0:T(8,128)(2,1)S(1)} %broadcast_select_fusion.4, bf16[2,64,7,128]{3,1,2,0:T(8,128)(2,1)} %get-tuple-element.466, s32[]{:T(128)S(6)} %copy.108, pred[2,128]{1,0:T(4,128)(4,1)S(1)} %add_compare_fusion.4), kind=kOutput, calls=%fused_computation.105.clone.1 | convolution fusion | flops 29817536 | bytes 644868 | tf_op jit(solution)/shard_map/while/body/eval_jaxpr/tgd,knd->tgkn/dot_general | solution.py:51
  31.1 1.7 %gather_fusion = bf16[2,128,256]{2,1,0:T(8,128)(2,1)S(1)} fusion(bf16[12,128,256]{2,1,0:T(8,128)(2,1)} %get-tuple-element.468, s32[1024]{0:T(1024)S(1)} %pad_clamp_fusion.4), kind=kCustom, calls=%fused_computation.clone.clone.1 | custom fusion | bytes 262152 | tf_op jit(solution)/shard_map/while/body/eval_jaxpr/jit(_take)/gather | solution.py:78
  32.9 1.4 %fusion.68 = (f32[64,7,2]{0,2,1:T(2,128)S(1)}, f32[64,7]{0,1:T(8,128)S(1)}, f32[64,7,2,128]{3,0,2,1:T(8,128)S(1)}) fusion(bf16[2,128,256]{2,1,0:T(8,128)(2,1)S(1)} %broadcast_select_fusion.4, bf16[2,64,7,128]{3,1,2,0:T(8,128)(2,1)} %get-tuple-element.466, s32[]{:T(128)S(6)} %copy.108, pred[2,128]{1,0:T(4,128)(4,1)S(1)} %add_compare_fusion.4), kind=kOutput, calls=%fused_computation.105.clone.1 | convolution fusion | flops 29817536 | bytes 644868 | tf_op jit(solution)/shard_map/while/body/eval_jaxpr/tgd,knd->tgkn/dot_general | solution.py:51
  41.3 1.4 %slice_reduce_fusion = s32[2]{0:T(128)} fusion(s32[2,9]{1,0:T(2,128)} %collective-permute-done), kind=kLoop, calls=%fused_computation.99 | loop fusion | bytes 16 | tf_op jit(solution)/shard_map/slice | solution.py:97
  46.7 23.4 %while.31 = (s32[]{:T(128)}, f32[2,64,7]{1,2,0:T(8,128)}, f32[2,64,7]{1,2,0:T(8,128)}, f32[2,64,7,128]{3,1,2,0:T(8,128)}, s32[2]{0:T(128)}, /*index=5*/bf16[2,64...) while((s32[]{:T(128)}, f32[2,64,7]{1,2,0:T(8,128)}, ...), condition=%wide.region_13.14_spmd.clone, body=%wide.region_7.13_spmd.clone.sunk | while | flops 180089152 | bytes 11682033 | solution.py:82
  46.7 1.3 %dynamic_slice.70 = s32[1]{0:T(128)} dynamic-slice(s32[2]{0:T(128)} %get-tuple-element.435, s32[]{:T(128)S(6)} %copy.96), dynamic_slice_sizes={1} | dynamic-slice | bytes 12 | tf_op jit(solution)/shard_map/while/body/jit(dynamic_index_in_dim)/dynamic_slice | solution.py:82
  48.0 1.4 %add_compare_fusion.5 = pred[6,128]{1,0:T(8,128)(4,1)S(1)} fusion(s32[6]{0:T(128)} %get-tuple-element.439, s32[]{:T(128)} %bitcast.153), kind=kLoop, calls=%fused_computation.49.clone.1 | loop fusion | flops 1536 | bytes 796 | tf_op jit(solution)/shard_map/while/body/eval_jaxpr/lt | solution.py:79
  51.4 2.5 %gather_fusion.1 = bf16[6,128,256]{2,1,0:T(8,128)(2,1)} fusion(bf16[12,128,256]{2,1,0:T(8,128)(2,1)} %get-tuple-element.438, s32[1024]{0:T(1024)S(1)} %pad_clamp_fusion.5), kind=kCustom, calls=%fused_computation.1.clone.clone.1 | custom fusion | bytes 786456 | tf_op jit(solution)/shard_map/while/body/eval_jaxpr/jit(_take)/gather | solution.py:78
  59.7 1.4 %add_compare_fusion.5 = pred[6,128]{1,0:T(8,128)(4,1)S(1)} fusion(s32[6]{0:T(128)} %get-tuple-element.439, s32[]{:T(128)} %bitcast.153), kind=kLoop, calls=%fused_computation.49.clone.1 | loop fusion | flops 1536 | bytes 796 | tf_op jit(solution)/shard_map/while/body/eval_jaxpr/lt | solution.py:79
  63.1 2.5 %gather_fusion.1 = bf16[6,128,256]{2,1,0:T(8,128)(2,1)} fusion(bf16[12,128,256]{2,1,0:T(8,128)(2,1)} %get-tuple-element.438, s32[1024]{0:T(1024)S(1)} %pad_clamp_fusion.5), kind=kCustom, calls=%fused_computation.1.clone.clone.1 | custom fusion | bytes 786456 | tf_op jit(solution)/shard_map/while/body/eval_jaxpr/jit(_take)/gather | solution.py:78
  70.0 11.4 %collective-permute-start.3 = (f32[2,64,7,128]{3,1,2,0:T(8,128)}, f32[2,64,7,128]{3,1,2,0:T(8,128)}, u32[]{:S(2)}, u32[]{:S(2)}) collective-permute-start(f32[2,64,7,128]{3,1,2,0:T(8,128)} %get-tuple-element.103), channel_id=1, source_target_pairs={{4,0},{8,4},{12,8},{16,12},{20,16},{24,20},{28,24},{32,28},{36,32}... | collective-permute-start | bytes 1376264 | tf_op jit(solution)/shard_map/ppermute | solution.py:15
  81.5 1.4 %convolution_convert_fusion = bf16[2,64,256]{2,1,0:T(8,128)(2,1)} fusion(bf16[2,64,256]{2,1,0:T(8,128)(2,1)S(1)} %bitcast.158, f32[2,64]{1,0:T(2,128)} %bitcast.160, f32[2,64]{1,0:T(2,128)} %broadcast_add_fusion), kind=kOutput, calls=%fused_computation.58 | convolution fusion | flops 4243456 | bytes 132096 | tf_op jit(solution)/shard_map/rsm,rmc->rsc/dot_general | solution.py:124
  82.9 2.6 %collective-permute-start.2 = (f32[2,64,7]{1,2,0:T(8,128)}, f32[2,64,7]{1,2,0:T(8,128)S(1)}, u32[]{:S(2)}, u32[]{:S(2)}) collective-permute-start(f32[2,64,7]{1,2,0:T(8,128)} %get-tuple-element.101), channel_id=1, source_target_pairs={{4,0},{8,4},{12,8},{16,12},{20,16},{24,20},{28,24},{32,28},{36,32}... | collective-permute-start | bytes 10760 | tf_op jit(solution)/shard_map/ppermute | solution.py:15
  85.5 3.7 %collective-permute-start.4 = (f32[2,64,7]{1,2,0:T(8,128)}, f32[2,64,7]{1,2,0:T(8,128)S(1)}, u32[]{:S(2)}, u32[]{:S(2)}) collective-permute-start(f32[2,64,7]{1,2,0:T(8,128)} %get-tuple-element.105), channel_id=1, source_target_pairs={{4,0},{8,4},{12,8},{16,12},{20,16},{24,20},{28,24},{32,28},{36,32}... | collective-permute-start | bytes 10760 | tf_op jit(solution)/shard_map/ppermute | solution.py:15
  90.8 1.9 %divide_convert_fusion = bf16[2,64,7,128]{3,1,2,0:T(8,128)(2,1)S(1)} fusion(f32[2,64,7,128]{3,1,2,0:T(8,128)} %fusion.26, f32[2,64,7,128]{3,1,2,0:T(8,128)} %collective-permute-done.3, f32[2,64,7,128]{3,1,2,0:T(8,128)} %get-tuple-element.102, f32[2,64,7]{1,2,0:T(8,128)S(1)} %get-tuple-element.250, f32[2,64,7]{1,2,0:T(8,128)S(1)} %get-tuple-element.254, ...), kind=kLoop, calls=%fused_computation.65 | loop fusion | flops 917504 | bytes 1623552 | tf_op jit(solution)/shard_map/convert_element_type | solution.py:109
  92.9 1.6 %fusion.21 = f32[128,1792]{1,0:T(8,128)} fusion(bf16[896,1792]{1,0:T(8,128)(2,1)S(1)} %copy-done, bf16[16,8,7,128]{3,2,1,0:T(8,128)(2,1)S(1)} %bitcast.155), kind=kOutput, calls=%fused_computation.68 | convolution fusion | flops 411041792 | bytes 4358144 | tf_op jit(solution)/shard_map/dot_general | solution.py:113
  94.5 26.9 %all-reduce.1 = bf16[128,1792]{1,0:T(8,128)(2,1)} all-reduce(f32[128,1792]{1,0:T(8,128)} %fusion.21), channel_id=1, replica_groups=mesh['req'=128,'tp'=4] {'tp'}, use_global_device_ids=true, to_apply=%region_16.17 | all-reduce | flops 229376 | bytes 1376256 | tf_op jit(solution)/shard_map/psum | solution.py:113
  121.4 1.6 %dynamic-slice_convert_fusion = bf16[32,1792]{1,0:T(8,128)(2,1)} fusion(bf16[128,1792]{1,0:T(8,128)(2,1)} %all-reduce.1, s32[]{:T(128)S(6)} %select_n.66), kind=kLoop, calls=%fused_computation.71 | loop fusion | bytes 229380 | tf_op jit(solution)/shard_map/convert_element_type | solution.py:115
  (138 shorter events, 45.8 us)
Async XLA Ops:
  0.6 92.2 %copy-start = (bf16[896,1792]{1,0:T(8,128)(2,1)S(1)}, bf16[896,1792]{1,0:T(8,128)(2,1)}, u32[]{:S(2)}) copy-start(bf16[896,1792]{1,0:T(8,128)(2,1)} %param.19) | copy-start | bytes 9633796
  2.9 37.1 %collective-permute-start = (s32[2,9]{1,0:T(2,128)}, s32[2,9]{1,0:T(2,128)}, u32[]{:S(2)}, u32[]{:S(2)}) collective-permute-start(s32[2,9]{1,0:T(2,128)} %pad_add_fusion), channel_id=1, source_target_pairs={{508,0},{0,4},{4,8},{8,12},{12,16},{16,20},{20,24},{24,28},{28,32}... | collective-permute-start | bytes 224 | tf_op jit(solution)/shard_map/ppermute | solution.py:15
  4.8 37.8 %collective-permute-start.1 = (bf16[128,896]{1,0:T(8,128)(2,1)}, bf16[128,896]{1,0:T(8,128)(2,1)}, u32[]{:S(2)}, u32[]{:S(2)}) collective-permute-start(bf16[128,896]{1,0:T(8,128)(2,1)} %param.12), channel_id=1, source_target_pairs={{508,0},{0,4},{4,8},{8,12},{12,16},{16,20},{20,24},{24,28},{28,32}... | collective-permute-start | bytes 688136 | tf_op jit(solution)/shard_map/ppermute | solution.py:15
  18.5 17.2 %copy-start.6 = (bf16[128,1,256]{2,0,1:T(8,128)(2,1)S(1)}, bf16[128,1,256]{2,0,1:T(8,128)(2,1)}, u32[]{:S(2)}) copy-start(bf16[128,1,256]{2,0,1:T(8,128)(2,1)} %param.13) | copy-start | bytes 196612
  24.2 2.1 %copy-start.2 = (f32[2,64,7,128]{3,1,2,0:T(8,128)S(1)}, f32[2,64,7,128]{3,1,2,0:T(8,128)}, u32[]{:S(2)}) copy-start(f32[2,64,7,128]{3,1,2,0:T(8,128)} %get-tuple-element.454) | copy-start | bytes 1376260 | tf_op jit(solution)/shard_map/while
  32.8 2.1 %copy-start.2 = (f32[2,64,7,128]{3,1,2,0:T(8,128)S(1)}, f32[2,64,7,128]{3,1,2,0:T(8,128)}, u32[]{:S(2)}) copy-start(f32[2,64,7,128]{3,1,2,0:T(8,128)} %get-tuple-element.454) | copy-start | bytes 1376260 | tf_op jit(solution)/shard_map/while
  35.7 7.0 %copy-start.10 = (f32[2,64,7]{1,2,0:T(8,128)}, f32[2,64,7]{1,2,0:T(8,128)S(1)}, u32[]{:S(2)}) copy-start(f32[2,64,7]{1,2,0:T(8,128)S(1)} %get-tuple-element.100) | copy-start | bytes 10756
  35.7 7.0 %copy-start.12 = (f32[2,64,7]{1,2,0:T(8,128)}, f32[2,64,7]{1,2,0:T(8,128)S(1)}, u32[]{:S(2)}) copy-start(f32[2,64,7]{1,2,0:T(8,128)S(1)} %get-tuple-element.104) | copy-start | bytes 10756
  35.7 3.1 %copy-start.18 = (f32[2,64]{1,0:T(2,128)S(1)}, f32[2,64]{1,0:T(2,128)}, u32[]{:S(2)}) copy-start(f32[2,64]{1,0:T(2,128)} %reduce_sum.73) | copy-start | bytes 1540
  37.0 1.8 %copy-start.8 = (f32[2,64,7]{1,2,0:T(8,128)}, f32[2,64,7]{1,2,0:T(8,128)S(1)}, u32[]{:S(2)}) copy-start(f32[2,64,7]{1,2,0:T(8,128)S(1)} %get-tuple-element.263) | copy-start | bytes 10756
  46.7 42.5 %copy-start.9 = (f32[2,64,7]{1,2,0:T(8,128)S(1)}, f32[2,64,7]{1,2,0:T(8,128)}, u32[]{:S(2)}) copy-start(f32[2,64,7]{1,2,0:T(8,128)} %copy-done.8) | copy-start | bytes 10756
  46.7 44.1 %copy-start.11 = (f32[2,64,7]{1,2,0:T(8,128)S(1)}, f32[2,64,7]{1,2,0:T(8,128)}, u32[]{:S(2)}) copy-start(f32[2,64,7]{1,2,0:T(8,128)} %copy-done.10) | copy-start | bytes 10756
  46.7 44.1 %copy-start.13 = (f32[2,64,7]{1,2,0:T(8,128)S(1)}, f32[2,64,7]{1,2,0:T(8,128)}, u32[]{:S(2)}) copy-start(f32[2,64,7]{1,2,0:T(8,128)} %copy-done.12) | copy-start | bytes 10756
  46.7 8.3 %copy-start.7 = (bf16[2,64,7,128]{3,1,2,0:T(8,128)(2,1)S(1)}, bf16[2,64,7,128]{3,1,2,0:T(8,128)(2,1)}, u32[]{:S(2)}) copy-start(bf16[2,64,7,128]{3,1,2,0:T(8,128)(2,1)} %get-tuple-element.436) | copy-start | bytes 688132 | tf_op jit(solution)/shard_map/while
  56.5 1.0 copy-start.4
  56.6 1.0 copy-start.15
  56.6 1.0 copy-start.17
  58.4 8.3 %copy-start.7 = (bf16[2,64,7,128]{3,1,2,0:T(8,128)(2,1)S(1)}, bf16[2,64,7,128]{3,1,2,0:T(8,128)(2,1)}, u32[]{:S(2)}) copy-start(bf16[2,64,7,128]{3,1,2,0:T(8,128)(2,1)} %get-tuple-element.436) | copy-start | bytes 688132 | tf_op jit(solution)/shard_map/while
  68.2 1.0 copy-start.4
  68.3 1.0 copy-start.15
  68.3 1.0 copy-start.17
  70.0 20.7 %collective-permute-start.3 = (f32[2,64,7,128]{3,1,2,0:T(8,128)}, f32[2,64,7,128]{3,1,2,0:T(8,128)}, u32[]{:S(2)}, u32[]{:S(2)}) collective-permute-start(f32[2,64,7,128]{3,1,2,0:T(8,128)} %get-tuple-element.103), channel_id=1, source_target_pairs={{4,0},{8,4},{12,8},{16,12},{20,16},{24,20},{28,24},{32,28},{36,32}... | collective-permute-start | bytes 1376264 | tf_op jit(solution)/shard_map/ppermute | solution.py:15
  82.9 7.4 %collective-permute-start.2 = (f32[2,64,7]{1,2,0:T(8,128)}, f32[2,64,7]{1,2,0:T(8,128)S(1)}, u32[]{:S(2)}, u32[]{:S(2)}) collective-permute-start(f32[2,64,7]{1,2,0:T(8,128)} %get-tuple-element.101), channel_id=1, source_target_pairs={{4,0},{8,4},{12,8},{16,12},{20,16},{24,20},{28,24},{32,28},{36,32}... | collective-permute-start | bytes 10760 | tf_op jit(solution)/shard_map/ppermute | solution.py:15
  85.5 5.2 %collective-permute-start.4 = (f32[2,64,7]{1,2,0:T(8,128)}, f32[2,64,7]{1,2,0:T(8,128)S(1)}, u32[]{:S(2)}, u32[]{:S(2)}) collective-permute-start(f32[2,64,7]{1,2,0:T(8,128)} %get-tuple-element.105), channel_id=1, source_target_pairs={{4,0},{8,4},{12,8},{16,12},{20,16},{24,20},{28,24},{32,28},{36,32}... | collective-permute-start | bytes 10760 | tf_op jit(solution)/shard_map/ppermute | solution.py:15
  (9 other events, 7.4 us)
where the time goes:
time: 124 us; the launch traced here: 123 us
  local copies, waits for them, and re-layouts  31.3 us (25%)
  blocking collectives  26.9 us (22%)
  other arithmetic  25.1 us (20%)
  starting transfers between devices  23.1 us (19%)
  matrix products  14.8 us (12%)
    psum x1, blocking collectives, shards(): lax.psum(jnp.dot(attention, o_weight, preferred_element_type=jnp.float32)...  26.9 us
    ppermute x5, starting transfers between devices, from_behind(): return lax.ppermute(block, axis, route)  23.1 us
    gather x4, local copies, waits for them, and re-layouts, one_request(): pages = jnp.take(pool_slots, table_row, axis=0)  8.31 us
    lt x4, other arithmetic, one_request(): visible = positions < length  5.47 us
    dynamic_slice x4, local copies, waits for them, and re-layouts, sweep_all(): return lax.map(one_request, (query_rows, tables, lengths))  5.16 us
    select_n x8, other arithmetic, one_request(): pages = jnp.take(pool_slots, table_row, axis=0)  5.11 us
    dot_general x4, matrix products, pages_partial(): jnp.einsum('tgd,knd->tgkn', query_rows, pages[..., :head_dim], preferred_...  4.09 us
    while x36, local copies, waits for them, and re-layouts  4.06 us
  transfers between devices with their start and end apart: 5, of which 1 were waited for; matrix products, arithmetic and copies ran while one was open for 28% of the time, Pallas kernels for 0%

commit v1 on v0

--- a/solution.py
+++ b/solution.py
@@ -110,7 +110,10 @@
         .reshape(requests * tree_len, group_size * HEAD_SIZE)
     )
     rows_out = attention.shape[0] // lax.axis_size("tp")
-    whole_sum = lax.psum(jnp.dot(attention, o_weight, preferred_element_type=jnp.float32), "tp")
+    whole_sum = jnp.sum(
+        lax.all_gather(jnp.dot(attention, o_weight, preferred_element_type=jnp.float32), "tp"),
+        axis=0,
+    )
     summed = lax.dynamic_slice_in_dim(whole_sum, lax.axis_index("tp") * rows_out, rows_out, 0)
     projected = summed.astype(jnp.bfloat16)
     node_ids = jnp.arange(tree_len, dtype=jnp.int32)

time: 124 us -> 154 us (1.24)
  the two profiles are of different devices: /device:TPU:8 before, /device:TPU:1 now
where the time goes in v1:
time: 154 us; the launch traced here: 152 us
  waiting for transfers between devices  48.2 us (31%)
  local copies, waits for them, and re-layouts  28.2 us (18%)
  starting transfers between devices  23 us (15%)
  other arithmetic  22.4 us (15%)
  matrix products  16.2 us (11%)
  between operations  14.3 us (9%)
    all_gather x1, waiting for transfers between devices, shards(): lax.all_gather(jnp.dot(attention, o_weight, preferred_element_type=jnp.fl...  46.9 us
    ppermute x5, starting transfers between devices, from_behind(): return lax.ppermute(block, axis, route)  23 us
    gather x4, local copies, waits for them, and re-layouts, one_request(): pages = jnp.take(pool_slots, table_row, axis=0)  8.34 us
    dot_general x4, matrix products, pages_partial(): jnp.einsum('tgd,knd->tgkn', query_rows, pages[..., :head_dim], preferred_...  5.81 us
    select_n x8, other arithmetic, one_request(): pages = jnp.take(pool_slots, table_row, axis=0)  5.13 us
    lt x4, other arithmetic, one_request(): visible = positions < length  4.24 us
    while x24, local copies, waits for them, and re-layouts  4.15 us
    dynamic_slice x4, local copies, waits for them, and re-layouts, sweep_all(): return lax.map(one_request, (query_rows, tables, lengths))  3.88 us
  transfers between devices with their start and end apart: 6, of which 2 were waited for; matrix products, arithmetic and copies ran while one was open for 21% of the time, Pallas kernels for 0%

profile of v1, /device:TPU:1, one launch (start us, length us, event | category | flops | bytes accessed | tf_op | source)
XLA Modules:
  0.0 152.5 jit_solution(13797022251197125763)
XLA Ops:
  8.1 1.4 pad_add_fusion
  9.5 4.5 %collective-permute-start = (s32[2,9]{1,0:T(2,128)}, s32[2,9]{1,0:T(2,128)}, u32[]{:S(2)}, u32[]{:S(2)}) collective-permute-start(s32[2,9]{1,0:T(2,128)} %pad_add_fusion), channel_id=1, source_target_pairs={{508,0},{0,4},{4,8},{8,12},{12,16},{16,20},{20,24},{24,28},{28,32}... | collective-permute-start | bytes 224 | tf_op jit(solution)/shard_map/ppermute | solution.py:15
  14.0 1.9 %collective-permute-start.1 = (bf16[128,896]{1,0:T(8,128)(2,1)}, bf16[128,896]{1,0:T(8,128)(2,1)}, u32[]{:S(2)}, u32[]{:S(2)}) collective-permute-start(bf16[128,896]{1,0:T(8,128)(2,1)} %param.12), channel_id=1, source_target_pairs={{508,0},{0,4},{4,8},{8,12},{12,16},{16,20},{20,24},{24,28},{28,32}... | collective-permute-start | bytes 688136 | tf_op jit(solution)/shard_map/ppermute | solution.py:15
  22.7 17.6 %while.30 = (s32[]{:T(128)}, f32[2,64,7]{1,2,0:T(8,128)S(1)}, f32[2,64,7]{1,2,0:T(8,128)S(1)}, f32[2,64,7,128]{3,1,2,0:T(8,128)}, s32[2]{0:T(128)}, /*index=5*/b...) while((s32[]{:T(128)}, f32[2,64,7]{1,2,0:T(8,128)S(1)}, ...), condition=%wide.region_6.7_spmd.clone, body=%wide.region_0.6_spmd.clone.sunk | while | flops 59991572 | bytes 6568945 | solution.py:82
  23.4 1.7 %gather_fusion = bf16[2,128,256]{2,1,0:T(8,128)(2,1)S(1)} fusion(bf16[12,128,256]{2,1,0:T(8,128)(2,1)} %get-tuple-element.468, s32[1024]{0:T(1024)S(1)} %pad_clamp_fusion.4), kind=kCustom, calls=%fused_computation.clone.clone.1 | custom fusion | bytes 262152 | tf_op jit(solution)/shard_map/while/body/eval_jaxpr/jit(_take)/gather | solution.py:78
  26.0 1.3 dynamic_slice.66
  27.3 1.4 add_compare_fusion.4
  32.2 1.7 %gather_fusion = bf16[2,128,256]{2,1,0:T(8,128)(2,1)S(1)} fusion(bf16[12,128,256]{2,1,0:T(8,128)(2,1)} %get-tuple-element.468, s32[1024]{0:T(1024)S(1)} %pad_clamp_fusion.4), kind=kCustom, calls=%fused_computation.clone.clone.1 | custom fusion | bytes 262152 | tf_op jit(solution)/shard_map/while/body/eval_jaxpr/jit(_take)/gather | solution.py:78
  34.7 1.3 dynamic_slice.66
  36.1 1.4 add_compare_fusion.4
  40.3 2.6 %fusion.43 = (f32[2,64,7]{1,2,0:T(8,128)}, f32[2,64,7,64]{1,3,2,0:T(8,128)}) fusion(bf16[2,64,7,128]{3,1,2,0:T(8,128)(2,1)} %get-tuple-element.476, bf16[2,64,256]{2,1,0:T(8,128)(2,1)S(1)} %bitcast.158, pred[2,64,64]{1,2,0:T(8,128)(4,1)S(1)} %copy.52), kind=kOutput, calls=%fused_computation.107 | convolution fusion | flops 14851200 | bytes 511488 | tf_op jit(solution)/shard_map/vmap(tgd,nd->tgn)/dot_general | solution.py:29
  44.8 1.3 slice_reduce_fusion
  48.9 21.1 %while.31 = (s32[]{:T(128)}, f32[2,64,7]{1,2,0:T(8,128)S(1)}, f32[2,64,7]{1,2,0:T(8,128)S(1)}, f32[2,64,7,128]{3,1,2,0:T(8,128)}, s32[2]{0:T(128)}, /*index=5*/b...) while((s32[]{:T(128)}, f32[2,64,7]{1,2,0:T(8,128)S(1)}, ...), condition=%wide.region_13.14_spmd.clone, body=%wide.region_7.13_spmd.clone.sunk | while | flops 180089152 | bytes 10707729 | solution.py:82
  49.7 2.5 %gather_fusion.1 = bf16[6,128,256]{2,1,0:T(8,128)(2,1)} fusion(bf16[12,128,256]{2,1,0:T(8,128)(2,1)} %get-tuple-element.438, s32[1024]{0:T(1024)S(1)} %pad_clamp_fusion.5), kind=kCustom, calls=%fused_computation.1.clone.clone.1 | custom fusion | bytes 786456 | tf_op jit(solution)/shard_map/while/body/eval_jaxpr/jit(_take)/gather | solution.py:78
  55.3 1.6 %fusion.72 = (f32[64,7,6]{0,2,1:T(8,128)S(1)}, f32[64,7]{0,1:T(8,128)S(1)}, f32[64,7,6,128]{3,0,2,1:T(8,128)S(1)}) fusion(bf16[6,128,256]{2,1,0:T(8,128)(2,1)S(1)} %broadcast_select_fusion.5, bf16[2,64,7,128]{3,1,2,0:T(8,128)(2,1)} %get-tuple-element.436, s32[]{:T(128)} %get-tuple-element.421, pred[6,128]{1,0:T(8,128)(4,1)S(1)} %add_compare_fusion.5), kind=kOutput, calls=%fused_computation.106.clone.1 | convolution fusion | flops 89453504 | bytes 1701632 | tf_op jit(solution)/shard_map/while/body/eval_jaxpr/tgd,knd->tgkn/dot_general | solution.py:51
  60.2 2.5 %gather_fusion.1 = bf16[6,128,256]{2,1,0:T(8,128)(2,1)} fusion(bf16[12,128,256]{2,1,0:T(8,128)(2,1)} %get-tuple-element.438, s32[1024]{0:T(1024)S(1)} %pad_clamp_fusion.5), kind=kCustom, calls=%fused_computation.1.clone.clone.1 | custom fusion | bytes 786456 | tf_op jit(solution)/shard_map/while/body/eval_jaxpr/jit(_take)/gather | solution.py:78
  65.8 1.6 %fusion.72 = (f32[64,7,6]{0,2,1:T(8,128)S(1)}, f32[64,7]{0,1:T(8,128)S(1)}, f32[64,7,6,128]{3,0,2,1:T(8,128)S(1)}) fusion(bf16[6,128,256]{2,1,0:T(8,128)(2,1)S(1)} %broadcast_select_fusion.5, bf16[2,64,7,128]{3,1,2,0:T(8,128)(2,1)} %get-tuple-element.436, s32[]{:T(128)} %get-tuple-element.421, pred[6,128]{1,0:T(8,128)(4,1)S(1)} %add_compare_fusion.5), kind=kOutput, calls=%fused_computation.106.clone.1 | convolution fusion | flops 89453504 | bytes 1701632 | tf_op jit(solution)/shard_map/while/body/eval_jaxpr/tgd,knd->tgkn/dot_general | solution.py:51
  70.0 6.3 %collective-permute-start.3 = (f32[2,64,7,128]{3,1,2,0:T(8,128)}, f32[2,64,7,128]{3,1,2,0:T(8,128)S(1)}, u32[]{:S(2)}, u32[]{:S(2)}) collective-permute-start(f32[2,64,7,128]{3,1,2,0:T(8,128)} %get-tuple-element.103), channel_id=1, source_target_pairs={{4,0},{8,4},{12,8},{16,12},{20,16},{24,20},{28,24},{32,28},{36,32}... | collective-permute-start | bytes 1376264 | tf_op jit(solution)/shard_map/ppermute | solution.py:15
  77.6 7.7 %collective-permute-start.2 = (f32[2,64,7]{1,2,0:T(8,128)S(1)}, f32[2,64,7]{1,2,0:T(8,128)S(1)}, u32[]{:S(2)}, u32[]{:S(2)}) collective-permute-start(f32[2,64,7]{1,2,0:T(8,128)S(1)} %get-tuple-element.101), channel_id=1, source_target_pairs={{4,0},{8,4},{12,8},{16,12},{20,16},{24,20},{28,24},{32,28},{36,32}... | collective-permute-start | bytes 10760 | tf_op jit(solution)/shard_map/ppermute | solution.py:15
  85.4 2.5 %collective-permute-start.4 = (f32[2,64,7]{1,2,0:T(8,128)S(1)}, f32[2,64,7]{1,2,0:T(8,128)S(1)}, u32[]{:S(2)}, u32[]{:S(2)}) collective-permute-start(f32[2,64,7]{1,2,0:T(8,128)S(1)} %get-tuple-element.105), channel_id=1, source_target_pairs={{4,0},{8,4},{12,8},{16,12},{20,16},{24,20},{28,24},{32,28},{36,32}... | collective-permute-start | bytes 10760 | tf_op jit(solution)/shard_map/ppermute | solution.py:15
  91.3 1.6 %fusion.21 = f32[128,1792]{1,0:T(8,128)} fusion(bf16[896,1792]{1,0:T(8,128)(2,1)S(1)} %copy-done, bf16[16,8,7,128]{3,2,1,0:T(8,128)(2,1)S(1)} %bitcast.157), kind=kOutput, calls=%fused_computation.68 | convolution fusion | flops 411041792 | bytes 4358144 | tf_op jit(solution)/shard_map/dot_general | solution.py:114
  94.1 46.9 %all-gather.3.cloned.1.call-done = f32[512,1792]{1,0:T(8,128)} async-done(((f32[128,1792]{1,0:T(8,128)}), f32[512,1792]{1,0:T(8,128)}) %all-gather.3.cloned.1.call-update) | async-done | bytes 3670032 | tf_op jit(solution)/shard_map/all_gather | solution.py:114
  140.9 3.2 %reduce_sum.82 = bf16[128,1792]{1,0:T(8,128)(2,1)} reduce(f32[4,128,1792]{2,1,0:T(8,128)} %bitcast.156, f32[]{:T(128)} %constant.92.clone.1), dimensions={0}, to_apply=%region_16.17 | reduce | flops 688128 | bytes 4128772 | tf_op jit(solution)/shard_map/reduce_sum | solution.py:113
  144.1 1.6 %dynamic-slice_convert_fusion = bf16[32,1792]{1,0:T(8,128)(2,1)} fusion(bf16[128,1792]{1,0:T(8,128)(2,1)} %reduce_sum.82, s32[]{:T(128)S(6)} %select_n.66), kind=kLoop, calls=%fused_computation.71 | loop fusion | bytes 229380 | tf_op jit(solution)/shard_map/convert_element_type | solution.py:118
  (129 shorter events, 39.5 us)
Async XLA Ops:
  7.2 84.2 %copy-start = (bf16[896,1792]{1,0:T(8,128)(2,1)S(1)}, bf16[896,1792]{1,0:T(8,128)(2,1)}, u32[]{:S(2)}) copy-start(bf16[896,1792]{1,0:T(8,128)(2,1)} %param.19) | copy-start | bytes 9633796
  7.2 133.7 %all-gather.3.cloned.1.call-start = ((), (), s32[]{:S(2)}) async-start(), calls=%async_computation | async-start | bytes 4587520 | tf_op jit(solution)/shard_map/all_gather | solution.py:114
  9.5 34.0 %collective-permute-start = (s32[2,9]{1,0:T(2,128)}, s32[2,9]{1,0:T(2,128)}, u32[]{:S(2)}, u32[]{:S(2)}) collective-permute-start(s32[2,9]{1,0:T(2,128)} %pad_add_fusion), channel_id=1, source_target_pairs={{508,0},{0,4},{4,8},{8,12},{12,16},{16,20},{20,24},{24,28},{28,32}... | collective-permute-start | bytes 224 | tf_op jit(solution)/shard_map/ppermute | solution.py:15
  14.0 32.2 %collective-permute-start.1 = (bf16[128,896]{1,0:T(8,128)(2,1)}, bf16[128,896]{1,0:T(8,128)(2,1)}, u32[]{:S(2)}, u32[]{:S(2)}) collective-permute-start(bf16[128,896]{1,0:T(8,128)(2,1)} %param.12), channel_id=1, source_target_pairs={{508,0},{0,4},{4,8},{8,12},{12,16},{16,20},{20,24},{24,28},{28,32}... | collective-permute-start | bytes 688136 | tf_op jit(solution)/shard_map/ppermute | solution.py:15
  22.7 17.6 %copy-start.6 = (bf16[128,1,256]{2,0,1:T(8,128)(2,1)S(1)}, bf16[128,1,256]{2,0,1:T(8,128)(2,1)}, u32[]{:S(2)}) copy-start(bf16[128,1,256]{2,0,1:T(8,128)(2,1)} %param.13) | copy-start | bytes 196612
  25.1 5.6 %copy-start.1 = (f32[2,64,7,128]{3,1,2,0:T(8,128)S(1)}, f32[2,64,7,128]{3,1,2,0:T(8,128)}, u32[]{:S(2)}) copy-start(f32[2,64,7,128]{3,1,2,0:T(8,128)} %get-tuple-element.454) | copy-start | bytes 1376260 | tf_op jit(solution)/shard_map/while
  33.9 5.6 %copy-start.1 = (f32[2,64,7,128]{3,1,2,0:T(8,128)S(1)}, f32[2,64,7,128]{3,1,2,0:T(8,128)}, u32[]{:S(2)}) copy-start(f32[2,64,7,128]{3,1,2,0:T(8,128)} %get-tuple-element.454) | copy-start | bytes 1376260 | tf_op jit(solution)/shard_map/while
  40.3 5.9 %copy-start.9 = (f32[2,64,7]{1,2,0:T(8,128)}, f32[2,64,7]{1,2,0:T(8,128)S(1)}, u32[]{:S(2)}) copy-start(f32[2,64,7]{1,2,0:T(8,128)S(1)} %get-tuple-element.100) | copy-start | bytes 10756
  40.3 5.9 %copy-start.11 = (f32[2,64,7]{1,2,0:T(8,128)}, f32[2,64,7]{1,2,0:T(8,128)S(1)}, u32[]{:S(2)}) copy-start(f32[2,64,7]{1,2,0:T(8,128)S(1)} %get-tuple-element.104) | copy-start | bytes 10756
  48.9 27.4 %copy-start.7 = (bf16[128,1,256]{2,0,1:T(8,128)(2,1)S(1)}, bf16[128,1,256]{2,0,1:T(8,128)(2,1)}, u32[]{:S(2)}) copy-start(bf16[128,1,256]{2,0,1:T(8,128)(2,1)} %param.13) | copy-start | bytes 196612
  48.9 27.4 %copy-start.8 = (f32[2,64,7]{1,2,0:T(8,128)S(1)}, f32[2,64,7]{1,2,0:T(8,128)}, u32[]{:S(2)}) copy-start(f32[2,64,7]{1,2,0:T(8,128)} %get-tuple-element.263) | copy-start | bytes 10756
  48.9 5.0 %copy-start.15 = (s32[2]{0:T(128)S(1)}, s32[2]{0:T(128)}, u32[]{:S(2)}) copy-start(s32[2]{0:T(128)} %get-tuple-element.435) | copy-start | bytes 28 | tf_op jit(solution)/shard_map/while
  49.0 5.6 %copy-start.13 = (s32[6]{0:T(128)S(1)}, s32[6]{0:T(128)}, u32[]{:S(2)}) copy-start(s32[6]{0:T(128)} %get-tuple-element.439) | copy-start | bytes 76 | tf_op jit(solution)/shard_map/while
  57.7 1.0 copy-start.4
  59.5 5.0 %copy-start.15 = (s32[2]{0:T(128)S(1)}, s32[2]{0:T(128)}, u32[]{:S(2)}) copy-start(s32[2]{0:T(128)} %get-tuple-element.435) | copy-start | bytes 28 | tf_op jit(solution)/shard_map/while
  59.5 5.6 %copy-start.13 = (s32[6]{0:T(128)S(1)}, s32[6]{0:T(128)}, u32[]{:S(2)}) copy-start(s32[6]{0:T(128)} %get-tuple-element.439) | copy-start | bytes 76 | tf_op jit(solution)/shard_map/while
  68.2 1.0 copy-start.4
  70.0 20.3 %copy-start.10 = (f32[2,64,7]{1,2,0:T(8,128)S(1)}, f32[2,64,7]{1,2,0:T(8,128)}, u32[]{:S(2)}) copy-start(f32[2,64,7]{1,2,0:T(8,128)} %copy-done.9) | copy-start | bytes 10756
  70.0 20.3 %copy-start.12 = (f32[2,64,7]{1,2,0:T(8,128)S(1)}, f32[2,64,7]{1,2,0:T(8,128)}, u32[]{:S(2)}) copy-start(f32[2,64,7]{1,2,0:T(8,128)} %copy-done.11) | copy-start | bytes 10756
  70.0 20.3 %copy-start.3 = (f32[2,64,7,128]{3,1,2,0:T(8,128)S(1)}, f32[2,64,7,128]{3,1,2,0:T(8,128)}, u32[]{:S(2)}) copy-start(f32[2,64,7,128]{3,1,2,0:T(8,128)} %get-tuple-element.102) | copy-start | bytes 1376260
  70.0 20.3 %collective-permute-start.3 = (f32[2,64,7,128]{3,1,2,0:T(8,128)}, f32[2,64,7,128]{3,1,2,0:T(8,128)S(1)}, u32[]{:S(2)}, u32[]{:S(2)}) collective-permute-start(f32[2,64,7,128]{3,1,2,0:T(8,128)} %get-tuple-element.103), channel_id=1, source_target_pairs={{4,0},{8,4},{12,8},{16,12},{20,16},{24,20},{28,24},{32,28},{36,32}... | collective-permute-start | bytes 1376264 | tf_op jit(solution)/shard_map/ppermute | solution.py:15
  77.6 11.4 %collective-permute-start.2 = (f32[2,64,7]{1,2,0:T(8,128)S(1)}, f32[2,64,7]{1,2,0:T(8,128)S(1)}, u32[]{:S(2)}, u32[]{:S(2)}) collective-permute-start(f32[2,64,7]{1,2,0:T(8,128)S(1)} %get-tuple-element.101), channel_id=1, source_target_pairs={{4,0},{8,4},{12,8},{16,12},{20,16},{24,20},{28,24},{32,28},{36,32}... | collective-permute-start | bytes 10760 | tf_op jit(solution)/shard_map/ppermute | solution.py:15
  85.4 5.0 %collective-permute-start.4 = (f32[2,64,7]{1,2,0:T(8,128)S(1)}, f32[2,64,7]{1,2,0:T(8,128)S(1)}, u32[]{:S(2)}, u32[]{:S(2)}) collective-permute-start(f32[2,64,7]{1,2,0:T(8,128)S(1)} %get-tuple-element.105), channel_id=1, source_target_pairs={{4,0},{8,4},{12,8},{16,12},{20,16},{24,20},{28,24},{32,28},{36,32}... | collective-permute-start | bytes 10760 | tf_op jit(solution)/shard_map/ppermute | solution.py:15
  91.3 1.7 %copy-start.14 = (s32[2]{0:T(128)S(1)}, s32[2]{0:T(128)}, u32[]{:S(2)}) copy-start(s32[2]{0:T(128)} %param.18) | copy-start | bytes 28
  (4 other events, 3.1 us)
Sparse Core Ops, SparseCore 0:
  93.1 47.8 all-gather.2
